TPU v7x, 512 devices: a whole 4x8x8 slice. The times are simulated.
512 devices in a mesh: space: 32 (over y, x_lo, core), modes: 16 (over z, x_hi).
Axes of the slice: x: 4 (x_hi: 2, x_lo: 2; x = x_hi * 2 + x_lo), y: 8, z: 8, core: 2. Of those that a mesh axis runs over, the one named last changes fastest.
Arguments:
- rhs: bfloat16 [2, 256, 512, 512], P(None, 'modes', 'space'), may hold values from -6 to 6
- initial: bfloat16 [2, 256, 512, 512], P(None, 'modes', 'space'), may hold values from -6 to 6
- region: int32 [512, 512], P('space'), may hold values from 0 to 7
- base_table: float32 [2, 8], replicated, may hold values from 0.5 to 4
- term_table: float32 [2, 3, 8], replicated, may hold values from -0.3 to 0.3
- galerkin: bfloat16 [3, 256, 256], replicated, may hold values from -0.375 to 0.375
- block_mask: int32 [3, 16, 16], replicated, may hold values from 0 to 1, as said below
- block_inverse: float32 [16, 16, 16], P('modes'), as said below
Outputs:
- solution: float32 [2, 256, 512, 512], P(None, 'modes', 'space')
Inputs may be any that keep to these rules, and one draw needn't show every extreme that they name: `block_mask`: each mode block is coupled with itself by every term, and some pairs of mode blocks are not coupled. `block_inverse`: blocks near the identity, off-diagonal entries at most 0.3 in magnitude.
All inputs are finite; a program needn't handle non-finite values.
Results may differ from a plain program's by a relative error of at most 0.0017.
Values may be sent and summed in bfloat16 or wider, within the bound.
No kernel may reach another device: no remote copies, remote signals or barrier semaphores. Data moves between devices by JAX's collectives and lax.ppermute only.
A program may use at most 64 MiB of HBM per device.

v0:
```python
import jax
import jax.numpy as jnp
from jax import lax
from jax.sharding import PartitionSpec as P

SWEEPS = 2


def with_halo(block, sides, width):
    for axis, dim in sides:
        count = lax.axis_size(axis)
        forward = [(i, i + 1) for i in range(count - 1)]
        forward.append((count - 1, 0))
        backward = [(target, source) for source, target in forward]
        low = lax.ppermute(
            lax.slice_in_dim(block, block.shape[dim] - width, None, axis=dim), axis, forward
        )
        high = lax.ppermute(lax.slice_in_dim(block, 0, width, axis=dim), axis, backward)
        block = jnp.concatenate([low, block, high], axis=dim)
    return block


def lookup(table, region):
    total = jnp.zeros(table.shape[:-1] + region.shape, jnp.float32)
    for which in range(table.shape[-1]):
        total = total + table[..., which, None, None] * (region == which).astype(jnp.float32)
    return total


def laplace_padded(padded):
    center = padded[..., 1:-1, :]
    zeros = jnp.zeros(center.shape[:-1] + (1,), jnp.float32)
    right = jnp.concatenate([center[..., 1:], zeros], -1)
    left = jnp.concatenate([zeros, center[..., :-1]], -1)
    return 4.0 * center - padded[..., 2:, :] - padded[..., :-2, :] - right - left


def body(rhs, initial, region, base_table, term_table, galerkin, block_mask, block_inverse):
    terms = galerkin.shape[0]
    modes_all = galerkin.shape[1]
    blocks = block_mask.shape[1]
    width = modes_all // blocks
    shaped = galerkin.reshape(terms, blocks, width, blocks, width)
    coupling = (shaped * block_mask[:, :, None, :, None].astype(jnp.bfloat16)).reshape(
        terms, modes_all, modes_all
    )
    base = lookup(base_table, region)
    coef = lookup(term_table, region)
    rhs_float = rhs.astype(jnp.float32)
    inverse_base = 1.0 / (4.0 * base[:, None])
    u_field = initial.astype(jnp.float32)
    for sweep in range(SWEEPS):
        padded = with_halo(u_field, (("space", 2),), 1)
        local = base[:, None] * laplace_padded(padded)
        rounded = lax.optimization_barrier(padded.astype(jnp.bfloat16)).astype(jnp.float32)
        lap_rounded = laplace_padded(rounded)
        tiles = (coef[:, :, None] * lap_rounded[:, None]).astype(jnp.bfloat16)
        mix_tiles = lax.all_to_all(tiles, "modes", split_axis=3, concat_axis=2, tiled=True)
        coupled = lax.all_to_all(
            jnp.einsum(
                "kij,fkjxy->fixy", coupling, mix_tiles, preferred_element_type=jnp.float32
            ).astype(jnp.bfloat16),
            "modes",
            split_axis=1,
            concat_axis=2,
            tiled=True,
        )
        resid = rhs_float - local - coupled.astype(jnp.float32)
        scaled = resid * inverse_base
        fields, modes_dev, cells_x, cells_y = scaled.shape
        grouped = scaled.reshape(fields, modes_dev // width, width, cells_x, cells_y)
        update = jnp.einsum(
            "bac,fbcxy->fbaxy", block_inverse, grouped, precision=lax.Precision.HIGHEST
        )
        u_field = u_field + 0.6 * update.reshape(fields, modes_dev, cells_x, cells_y)
    return u_field


def solution(mesh):
    in_specs = (
        P(None, "modes", "space", None),
        P(None, "modes", "space", None),
        P("space", None),
        P(),
        P(),
        P(),
        P(),
        P("modes", None, None),
    )
    out_specs = P(None, "modes", "space", None)
    return jax.shard_map(body, mesh=mesh, in_specs=in_specs, out_specs=out_specs, check_vma=False)
```

profile of v0, /device:TPU:16, one launch (start us, length us, event | category | flops | bytes accessed | tf_op | source)
XLA Modules:
  0.0 182.6 jit_solution(13610392275170002387)
XLA Ops:
  0.0 1.4 fusion.72
  1.5 1.9 %collective-permute-start.1 = (f32[2,16,1,512]{3,1,2,0:T(8,128)S(1)}, f32[2,16,1,512]{3,1,2,0:T(8,128)S(1)}, u32[]{:S(2)}, u32[]{:S(2)}) collective-permute-start(f32[2,16,1,512]{3,1,2,0:T(8,128)S(1)} %get-tuple-element.22), channel_id=1, source_target_pairs={{0,16},{16,32},{32,48},{48,64},{64,80},{80,96},{96,112},{112,128},... | collective-permute-start | bytes 196616 | tf_op jit(solution)/shard_map/ppermute | solution.py:15
  3.4 4.5 %collective-permute-start = (f32[2,16,1,512]{3,1,2,0:T(8,128)S(1)}, f32[2,16,1,512]{3,1,2,0:T(8,128)S(1)}, u32[]{:S(2)}, u32[]{:S(2)}) collective-permute-start(f32[2,16,1,512]{3,1,2,0:T(8,128)S(1)} %get-tuple-element.21), channel_id=1, source_target_pairs={{16,0},{32,16},{48,32},{64,48},{80,64},{96,80},{112,96},{128,112},... | collective-permute-start | bytes 196616 | tf_op jit(solution)/shard_map/ppermute | solution.py:18
  10.6 1.6 multiply_convert_fusion.1
  12.2 13.0 %all-to-all-start = ((bf16[2,3,16,16,512]{4,2,1,0,3:T(8,128)(2,1)}), bf16[2,3,16,16,512]{4,2,1,0,3:T(8,128)(2,1)S(1)}, u32[]{:S(2)}, u32[]{:S(2)}) async-start(bf16[2,3,16,16,512]{4,2,1,0,3:T(8,128)(2,1)} %multiply_convert_fusion.1), calls=%async_computation | async-start | bytes 3145728 | tf_op jit(solution)/shard_map/all_to_all | solution.py:58
  25.3 2.1 %mul.509 = bf16[3,16,16,16,16]{4,3,2,1,0:T(8,128)(2,1)} broadcast(bf16[3,16,16]{2,1,0:T(8,128)(2,1)S(1)} %convert_element_type.110), dimensions={0,1,3} | broadcast | bytes 394752 | tf_op jit(solution)/shard_map/mul | solution.py:44
  27.4 4.4 %mul.510 = bf16[3,256,256]{2,1,0:T(8,128)(2,1)S(1)} reshape(bf16[3,16,16,16,16]{4,3,2,1,0:T(8,128)(2,1)} %mul.509) | data formatting | bytes 786432 | tf_op jit(solution)/shard_map/mul | solution.py:44
  31.8 34.9 %all-to-all-done = bf16[2,3,16,16,512]{4,2,1,0,3:T(8,128)(2,1)S(1)} async-done(((bf16[2,3,16,16,512]{4,2,1,0,3:T(8,128)(2,1)}), bf16[2,3,16,16,512]{4,2,1,0,3:T(8,128)(2,1)S(1)}, u32[]{:S(2)}, u32[]{:S(2)}) %all-to-all-start) | async-done | bytes 1572896 | tf_op jit(solution)/shard_map/all_to_all | solution.py:58
  66.9 0.9 copy-done.21
  68.4 1.2 copy.85
  69.6 3.6 %all-to-all-start.1 = ((bf16[2,256,1,512]{3,0,2,1:T(2,128)(2,1)}), bf16[2,256,1,512]{3,0,2,1:T(2,128)(2,1)S(1)}, u32[]{:S(2)}, u32[]{:S(2)}) async-start(bf16[2,256,1,512]{3,0,2,1:T(2,128)(2,1)} %copy.85), calls=%async_computation.1 | async-start | bytes 1048576 | tf_op jit(solution)/shard_map/all_to_all | solution.py:59
  73.6 1.4 fusion.68
  75.0 17.1 %all-to-all-done.1 = bf16[2,256,1,512]{3,0,2,1:T(2,128)(2,1)S(1)} async-done(((bf16[2,256,1,512]{3,0,2,1:T(2,128)(2,1)}), bf16[2,256,1,512]{3,0,2,1:T(2,128)(2,1)S(1)}, u32[]{:S(2)}, u32[]{:S(2)}) %all-to-all-start.1) | async-done | bytes 524320 | tf_op jit(solution)/shard_map/all_to_all | solution.py:59
  92.1 3.3 %fusion.74 = (bf16[2,16,16,512]{3,1,2,0:T(8,128)(2,1)S(1)}, f32[2,16,16,512]{3,1,2,0:T(8,128)S(1)}) fusion(f32[2,16,16,512]{3,1,2,0:T(8,128)S(1)} %get-tuple-element.28, f32[1,16,16]{2,1,0:T(8,128)S(1)} %copy-done, f32[2,16,1,512]{3,1,2,0:T(8,128)} %copy-done.11, f32[2,16,1,512]{3,1,2,0:T(8,128)} %copy-done.12, ...), kind=kOutput, calls=%fused_computation.108 | convolution fusion | flops 54525952 | bytes 6026240 | tf_op jit(solution)/shard_map/bac,fbcxy->fbaxy/dot_general | solution.py:72
  95.5 1.9 %collective-permute-start.3 = (f32[2,16,1,512]{3,1,2,0:T(8,128)S(1)}, f32[2,16,1,512]{3,1,2,0:T(8,128)S(1)}, u32[]{:S(2)}, u32[]{:S(2)}) collective-permute-start(f32[2,16,1,512]{3,1,2,0:T(8,128)S(1)} %get-tuple-element.18), channel_id=1, source_target_pairs={{0,16},{16,32},{32,48},{48,64},{64,80},{80,96},{96,112},{112,128},... | collective-permute-start | bytes 196616 | tf_op jit(solution)/shard_map/ppermute | solution.py:15
  97.4 4.5 %collective-permute-start.2 = (f32[2,16,1,512]{3,1,2,0:T(8,128)S(1)}, f32[2,16,1,512]{3,1,2,0:T(8,128)S(1)}, u32[]{:S(2)}, u32[]{:S(2)}) collective-permute-start(f32[2,16,1,512]{3,1,2,0:T(8,128)S(1)} %get-tuple-element.17), channel_id=1, source_target_pairs={{16,0},{32,16},{48,32},{64,48},{80,64},{96,80},{112,96},{128,112},... | collective-permute-start | bytes 196616 | tf_op jit(solution)/shard_map/ppermute | solution.py:18
  102.0 1.8 %collective-permute-done.2 = f32[2,16,1,512]{3,1,2,0:T(8,128)S(1)} collective-permute-done((f32[2,16,1,512]{3,1,2,0:T(8,128)S(1)}, f32[2,16,1,512]{3,1,2,0:T(8,128)S(1)}, u32[]{:S(2)}, u32[]{:S(2)}) %collective-permute-start.2) | collective-permute-done | bytes 65568 | tf_op jit(solution)/shard_map/ppermute | solution.py:18
  105.6 45.6 %all_to_all.48 = bf16[2,3,16,16,512]{4,2,1,0,3:T(8,128)(2,1)S(1)} all-to-all(bf16[2,3,16,16,512]{4,2,1,0,3:T(8,128)(2,1)S(1)} %multiply_convert_fusion), channel_id=1, replica_groups=mesh['space'=32,'modes'=16] {'modes'}, dimensions={3} | all-to-all | bytes 3145728 | tf_op jit(solution)/shard_map/all_to_all | solution.py:58
  152.9 1.2 copy.90
  154.1 4.4 %all-to-all-start.3 = ((bf16[2,256,1,512]{3,0,2,1:T(2,128)(2,1)}), bf16[2,256,1,512]{3,0,2,1:T(2,128)(2,1)}, u32[]{:S(2)}, u32[]{:S(2)}) async-start(bf16[2,256,1,512]{3,0,2,1:T(2,128)(2,1)} %copy.90), calls=%async_computation.3 | async-start | bytes 1048576 | tf_op jit(solution)/shard_map/all_to_all | solution.py:59
  158.9 18.0 %all-to-all-done.3 = bf16[2,256,1,512]{3,0,2,1:T(2,128)(2,1)} async-done(((bf16[2,256,1,512]{3,0,2,1:T(2,128)(2,1)}), bf16[2,256,1,512]{3,0,2,1:T(2,128)(2,1)}, u32[]{:S(2)}, u32[]{:S(2)}) %all-to-all-start.3) | async-done | bytes 524320 | tf_op jit(solution)/shard_map/all_to_all | solution.py:59
  176.9 1.1 copy.91
  178.0 2.9 %fusion.1 = f32[2,16,16,512]{3,1,2,0:T(8,128)S(1)} fusion(f32[2,16,16,512]{3,1,2,0:T(8,128)S(1)} %get-tuple-element.46, f32[2,16,1,512]{3,1,2,0:T(8,128)S(1)} %copy-done.14, f32[2,16,1,512]{3,1,2,0:T(8,128)S(1)} %copy-done.16, bf16[2,16,16,1,512]{4,2,1,0,3:T(8,128)(2,1)S(1)} %bitcast.97, f32[2,16,16,511]{3,1,2,0:T(8,128)S(1)} %get-tuple-element.16, ...), kind=kOutput, calls=%fused_computation.4 | convolution fusion | flops 54263808 | bytes 5501952 | tf_op jit(solution)/shard_map/bac,fbcxy->fbaxy/dot_general | solution.py:72
  181.0 1.6 copy.92
  (81 shorter events, 7.6 us)
Async XLA Ops:
  0.0 92.1 %copy-start = (f32[1,16,16]{2,1,0:T(8,128)S(1)}, f32[1,16,16]{2,1,0:T(8,128)}, u32[]{:S(2)}) copy-start(f32[1,16,16]{2,1,0:T(8,128)} %param.15) | copy-start | bytes 3076
  0.0 7.9 %copy-start.19 = (s32[16,512]{1,0:T(8,128)S(1)}, s32[16,512]{1,0:T(8,128)}, u32[]{:S(2)}) copy-start(s32[16,512]{1,0:T(8,128)} %param.10) | copy-start | bytes 98308
  0.0 8.0 %copy-start.17 = (f32[2,3,8]{2,0,1:T(2,128)S(1)}, f32[2,3,8]{2,0,1:T(2,128)}, u32[]{:S(2)}) copy-start(f32[2,3,8]{2,0,1:T(2,128)} %param.12) | copy-start | bytes 580
  1.5 7.8 %collective-permute-start.1 = (f32[2,16,1,512]{3,1,2,0:T(8,128)S(1)}, f32[2,16,1,512]{3,1,2,0:T(8,128)S(1)}, u32[]{:S(2)}, u32[]{:S(2)}) collective-permute-start(f32[2,16,1,512]{3,1,2,0:T(8,128)S(1)} %get-tuple-element.22), channel_id=1, source_target_pairs={{0,16},{16,32},{32,48},{48,64},{64,80},{80,96},{96,112},{112,128},... | collective-permute-start | bytes 196616 | tf_op jit(solution)/shard_map/ppermute | solution.py:15
  3.4 6.4 %collective-permute-start = (f32[2,16,1,512]{3,1,2,0:T(8,128)S(1)}, f32[2,16,1,512]{3,1,2,0:T(8,128)S(1)}, u32[]{:S(2)}, u32[]{:S(2)}) collective-permute-start(f32[2,16,1,512]{3,1,2,0:T(8,128)S(1)} %get-tuple-element.21), channel_id=1, source_target_pairs={{16,0},{32,16},{48,32},{64,48},{80,64},{96,80},{112,96},{128,112},... | collective-permute-start | bytes 196616 | tf_op jit(solution)/shard_map/ppermute | solution.py:18
  8.0 2.3 %copy-start.3 = (f32[16,512]{1,0:T(8,128)}, f32[16,512]{1,0:T(8,128)S(1)}, u32[]{:S(2)}) copy-start(f32[16,512]{1,0:T(8,128)S(1)} %get-tuple-element.33) | copy-start | bytes 98308
  8.0 2.3 %copy-start.5 = (f32[16,512]{1,0:T(8,128)}, f32[16,512]{1,0:T(8,128)S(1)}, u32[]{:S(2)}) copy-start(f32[16,512]{1,0:T(8,128)S(1)} %get-tuple-element.34) | copy-start | bytes 98308
  8.0 2.3 %copy-start.7 = (f32[16,512]{1,0:T(8,128)}, f32[16,512]{1,0:T(8,128)S(1)}, u32[]{:S(2)}) copy-start(f32[16,512]{1,0:T(8,128)S(1)} %get-tuple-element.35) | copy-start | bytes 98308
  8.0 2.3 %copy-start.9 = (f32[16,512]{1,0:T(8,128)}, f32[16,512]{1,0:T(8,128)S(1)}, u32[]{:S(2)}) copy-start(f32[16,512]{1,0:T(8,128)S(1)} %get-tuple-element.36) | copy-start | bytes 98308
  12.2 13.0 %copy-start.20 = (s32[3,16,16]{2,1,0:T(8,128)S(1)}, s32[3,16,16]{2,1,0:T(8,128)}, u32[]{:S(2)}) copy-start(s32[3,16,16]{2,1,0:T(8,128)} %param.14) | copy-start | bytes 9220
  12.2 54.5 %all-to-all-start = ((bf16[2,3,16,16,512]{4,2,1,0,3:T(8,128)(2,1)}), bf16[2,3,16,16,512]{4,2,1,0,3:T(8,128)(2,1)S(1)}, u32[]{:S(2)}, u32[]{:S(2)}) async-start(bf16[2,3,16,16,512]{4,2,1,0,3:T(8,128)(2,1)} %multiply_convert_fusion.1), calls=%async_computation | async-start | bytes 3145728 | tf_op jit(solution)/shard_map/all_to_all | solution.py:58
  31.8 35.1 %copy-start.1 = (bf16[3,256,256]{2,1,0:T(8,128)(2,1)}, bf16[3,256,256]{2,1,0:T(8,128)(2,1)S(1)}, u32[]{:S(2)}) copy-start(bf16[3,256,256]{2,1,0:T(8,128)(2,1)S(1)} %mul.510) | copy-start | bytes 1179652
  68.4 4.8 %copy-start.18 = (f32[2,8]{1,0:T(2,128)S(1)}, f32[2,8]{1,0:T(2,128)}, u32[]{:S(2)}) copy-start(f32[2,8]{1,0:T(2,128)} %param.11) | copy-start | bytes 196
  68.4 5.1 %copy-start.4 = (f32[16,512]{1,0:T(8,128)S(1)}, f32[16,512]{1,0:T(8,128)}, u32[]{:S(2)}) copy-start(f32[16,512]{1,0:T(8,128)} %copy-done.3) | copy-start | bytes 98308
  68.4 5.1 %copy-start.6 = (f32[16,512]{1,0:T(8,128)S(1)}, f32[16,512]{1,0:T(8,128)}, u32[]{:S(2)}) copy-start(f32[16,512]{1,0:T(8,128)} %copy-done.5) | copy-start | bytes 98308
  68.4 5.1 %copy-start.8 = (f32[16,512]{1,0:T(8,128)S(1)}, f32[16,512]{1,0:T(8,128)}, u32[]{:S(2)}) copy-start(f32[16,512]{1,0:T(8,128)} %copy-done.7) | copy-start | bytes 98308
  68.4 5.1 %copy-start.10 = (f32[16,512]{1,0:T(8,128)S(1)}, f32[16,512]{1,0:T(8,128)}, u32[]{:S(2)}) copy-start(f32[16,512]{1,0:T(8,128)} %copy-done.9) | copy-start | bytes 98308
  69.6 22.5 %all-to-all-start.1 = ((bf16[2,256,1,512]{3,0,2,1:T(2,128)(2,1)}), bf16[2,256,1,512]{3,0,2,1:T(2,128)(2,1)S(1)}, u32[]{:S(2)}, u32[]{:S(2)}) async-start(bf16[2,256,1,512]{3,0,2,1:T(2,128)(2,1)} %copy.85), calls=%async_computation.1 | async-start | bytes 1048576 | tf_op jit(solution)/shard_map/all_to_all | solution.py:59
  95.5 6.5 %collective-permute-start.3 = (f32[2,16,1,512]{3,1,2,0:T(8,128)S(1)}, f32[2,16,1,512]{3,1,2,0:T(8,128)S(1)}, u32[]{:S(2)}, u32[]{:S(2)}) collective-permute-start(f32[2,16,1,512]{3,1,2,0:T(8,128)S(1)} %get-tuple-element.18), channel_id=1, source_target_pairs={{0,16},{16,32},{32,48},{48,64},{64,80},{80,96},{96,112},{112,128},... | collective-permute-start | bytes 196616 | tf_op jit(solution)/shard_map/ppermute | solution.py:15
  97.4 6.4 %collective-permute-start.2 = (f32[2,16,1,512]{3,1,2,0:T(8,128)S(1)}, f32[2,16,1,512]{3,1,2,0:T(8,128)S(1)}, u32[]{:S(2)}, u32[]{:S(2)}) collective-permute-start(f32[2,16,1,512]{3,1,2,0:T(8,128)S(1)} %get-tuple-element.17), channel_id=1, source_target_pairs={{16,0},{32,16},{48,32},{64,48},{80,64},{96,80},{112,96},{128,112},... | collective-permute-start | bytes 196616 | tf_op jit(solution)/shard_map/ppermute | solution.py:18
  102.0 1.9 %copy-start.13 = (f32[2,16,1,512]{3,1,2,0:T(8,128)}, f32[2,16,1,512]{3,1,2,0:T(8,128)S(1)}, u32[]{:S(2)}) copy-start(f32[2,16,1,512]{3,1,2,0:T(8,128)S(1)} %collective-permute-done.3) | copy-start | bytes 196612
  154.1 22.8 %all-to-all-start.3 = ((bf16[2,256,1,512]{3,0,2,1:T(2,128)(2,1)}), bf16[2,256,1,512]{3,0,2,1:T(2,128)(2,1)}, u32[]{:S(2)}, u32[]{:S(2)}) async-start(bf16[2,256,1,512]{3,0,2,1:T(2,128)(2,1)} %copy.90), calls=%async_computation.3 | async-start | bytes 1048576 | tf_op jit(solution)/shard_map/all_to_all | solution.py:59
  158.5 19.5 %copy-start.14 = (f32[2,16,1,512]{3,1,2,0:T(8,128)S(1)}, f32[2,16,1,512]{3,1,2,0:T(8,128)}, u32[]{:S(2)}) copy-start(f32[2,16,1,512]{3,1,2,0:T(8,128)} %copy-done.13) | copy-start | bytes 196612
  158.5 19.5 %copy-start.16 = (f32[2,16,1,512]{3,1,2,0:T(8,128)S(1)}, f32[2,16,1,512]{3,1,2,0:T(8,128)}, u32[]{:S(2)}) copy-start(f32[2,16,1,512]{3,1,2,0:T(8,128)} %copy-done.15) | copy-start | bytes 196612
  (6 other events, 5.4 us)
where the time goes:
time: 183 us
  waiting for transfers between devices  72.4 us (40%)
  blocking collectives  45.6 us (25%)
  starting transfers between devices  33.9 us (19%)
  local copies, waits for them, and re-layouts  18.1 us (10%)
  matrix products  7.59 us (4%)
  other arithmetic  4.48 us (2%)
    all_to_all x1, blocking collectives, body(): lax.all_to_all(tiles, 'modes', split_axis=3, concat_axis=2, tiled=True)  45.6 us
    all_to_all x2, waiting for transfers between devices, body(): lax.all_to_all(jnp.einsum('kij,fkjxy->fixy', coupling, mix_tiles, preferr...  35.1 us
    all_to_all x1, waiting for transfers between devices, body(): lax.all_to_all(tiles, 'modes', split_axis=3, concat_axis=2, tiled=True)  34.9 us
    all_to_all x1, starting transfers between devices, body(): lax.all_to_all(tiles, 'modes', split_axis=3, concat_axis=2, tiled=True)  13 us
    ppermute x2, starting transfers between devices, with_halo(): lax.ppermute(lax.slice_in_dim(block, 0, width, axis=dim), axis, backward)  9.08 us
    all_to_all x2, starting transfers between devices, body(): lax.all_to_all(jnp.einsum('kij,fkjxy->fixy', coupling, mix_tiles, preferr...  7.99 us
    mul x2, local copies, waits for them, and re-layouts, body(): shaped * block_mask[:, :, None, :, None].astype(jnp.bfloat16)  6.52 us
    dot_general x2, matrix products, body(): jnp.einsum('bac,fbcxy->fbaxy', block_inverse, grouped, precision=lax.Prec...  6.29 us
  transfers between devices with their start and end apart: 7, of which 5 were waited for; matrix products, arithmetic and copies ran while one was open for 5% of the time, Pallas kernels for 0%

commit v1 on v0

--- a/solution.py
+++ b/solution.py
@@ -2,6 +2,7 @@
 import jax.numpy as jnp
 from jax import lax
 from jax.sharding import PartitionSpec as P
+from jax.lax import all_to_all, axis_size
 
 SWEEPS = 2
 
@@ -56,14 +57,26 @@
         lap_rounded = laplace_padded(rounded)
         tiles = (coef[:, :, None] * lap_rounded[:, None]).astype(jnp.bfloat16)
         mix_tiles = lax.all_to_all(tiles, "modes", split_axis=3, concat_axis=2, tiled=True)
-        coupled = lax.all_to_all(
-            jnp.einsum(
-                "kij,fkjxy->fixy", coupling, mix_tiles, preferred_element_type=jnp.float32
-            ).astype(jnp.bfloat16),
-            "modes",
-            split_axis=1,
-            concat_axis=2,
-            tiled=True,
+        coupled = jnp.concatenate(
+            all_to_all(
+                jnp.stack(
+                    jnp.split(
+                        jnp.einsum(
+                            "kij,fkjxy->fixy",
+                            coupling,
+                            mix_tiles,
+                            preferred_element_type=jnp.float32,
+                        ).astype(jnp.bfloat16),
+                        axis_size("modes"),
+                        axis=1,
+                    ),
+                    axis=0,
+                ),
+                "modes",
+                0,
+                0,
+            ),
+            axis=2,
         )
         resid = rhs_float - local - coupled.astype(jnp.float32)
         scaled = resid * inverse_base

time: 183 us -> 202 us (1.10)
  local copies, waits for them, and re-layouts: 18.1 us -> 36.8 us
    unnamed x46 -> x82, local copies, waits for them, and re-layouts: 2.55 us -> 22.2 us
    convert_element_type x2 -> x0, local copies, waits for them, and re-layouts: 2.34 us -> none  [body(): coupled = lax.all_to_all(jnp.einsum('kij,fkjxy->fixy', coupling, mix_tile...]
  transfers between devices with their start and end apart: 7 -> 7, of which waited for: 5 -> 5; matrix products, arithmetic and copies ran while one was open for 5% -> 6% of each run, Pallas kernels for 0% -> 0%
where the time goes in v1:
time: 202 us; the launch traced here: 201 us
  waiting for transfers between devices  71 us (35%)
  blocking collectives  45.6 us (23%)
  local copies, waits for them, and re-layouts  36.8 us (18%)
  starting transfers between devices  33.9 us (17%)
  matrix products  7.73 us (4%)
  other arithmetic  5.6 us (3%)
    all_to_all x1, blocking collectives, body(): lax.all_to_all(tiles, 'modes', split_axis=3, concat_axis=2, tiled=True)  45.6 us
    all_to_all x1, waiting for transfers between devices, body(): lax.all_to_all(tiles, 'modes', split_axis=3, concat_axis=2, tiled=True)  35 us
    all_to_all x2, waiting for transfers between devices, body(): all_to_all(jnp.stack(jnp.split(jnp.einsum('kij,fkjxy->fixy', coupling, mi...  33.7 us
    unnamed x82, local copies, waits for them, and re-layouts  22.2 us
    all_to_all x1, starting transfers between devices, body(): lax.all_to_all(tiles, 'modes', split_axis=3, concat_axis=2, tiled=True)  13 us
    ppermute x2, starting transfers between devices, with_halo(): lax.ppermute(lax.slice_in_dim(block, 0, width, axis=dim), axis, backward)  9.08 us
    all_to_all x2, starting transfers between devices, body(): all_to_all(jnp.stack(jnp.split(jnp.einsum('kij,fkjxy->fixy', coupling, mi...  8.01 us
    dot_general x2, matrix products, body(): jnp.einsum('bac,fbcxy->fbaxy', block_inverse, grouped, precision=lax.Prec...  6.56 us
  transfers between devices with their start and end apart: 7, of which 5 were waited for; matrix products, arithmetic and copies ran while one was open for 6% of the time, Pallas kernels for 0%

profile of v1, /device:TPU:16, one launch (start us, length us, event | category | flops | bytes accessed | tf_op | source)
XLA Modules:
  0.0 201.3 jit_solution(17966568761862463102)
XLA Ops:
  0.0 1.4 fusion.73
  1.5 1.9 collective-permute-start.1
  3.4 4.5 %collective-permute-start = (f32[2,16,1,512]{3,1,0,2:T(8,128)S(1)}, f32[2,16,1,512]{3,1,0,2:T(8,128)S(1)}, u32[]{:S(2)}, u32[]{:S(2)}) collective-permute-start(f32[2,16,1,512]{3,1,0,2:T(8,128)S(1)} %get-tuple-element.21), channel_id=1, source_target_pairs={{16,0},{32,16},{48,32},{64,48},{80,64},{96,80},{112,96},{128,112},... | collective-permute-start | bytes 196616 | tf_op jit(solution)/shard_map/ppermute | solution.py:19
  11.1 1.7 multiply_convert_fusion.1
  12.8 13.0 %all-to-all-start = ((bf16[2,3,16,16,512]{4,2,1,0,3:T(8,128)(2,1)}), bf16[2,3,16,16,512]{4,2,1,0,3:T(8,128)(2,1)S(1)}, u32[]{:S(2)}, u32[]{:S(2)}) async-start(bf16[2,3,16,16,512]{4,2,1,0,3:T(8,128)(2,1)} %multiply_convert_fusion.1), calls=%async_computation | async-start | bytes 3145728 | tf_op jit(solution)/shard_map/all_to_all | solution.py:59
  25.8 2.1 %mul.509 = bf16[3,16,16,16,16]{4,3,2,1,0:T(8,128)(2,1)} broadcast(bf16[3,16,16]{2,1,0:T(8,128)(2,1)S(1)} %convert_element_type.104), dimensions={0,1,3} | broadcast | bytes 394752 | tf_op jit(solution)/shard_map/mul | solution.py:45
  27.9 4.4 %mul.510 = bf16[3,256,256]{2,1,0:T(8,128)(2,1)S(1)} reshape(bf16[3,16,16,16,16]{4,3,2,1,0:T(8,128)(2,1)} %mul.509) | data formatting | bytes 786432 | tf_op jit(solution)/shard_map/mul | solution.py:45
  32.4 35.0 %all-to-all-done = bf16[2,3,16,16,512]{4,2,1,0,3:T(8,128)(2,1)S(1)} async-done(((bf16[2,3,16,16,512]{4,2,1,0,3:T(8,128)(2,1)}), bf16[2,3,16,16,512]{4,2,1,0,3:T(8,128)(2,1)S(1)}, u32[]{:S(2)}, u32[]{:S(2)}) %all-to-all-start) | async-done | bytes 1572896 | tf_op jit(solution)/shard_map/all_to_all | solution.py:59
  67.4 0.9 copy-done.4
  78.8 3.6 %all-to-all-start.1 = ((bf16[16,2,16,1,512]{4,2,1,3,0:T(8,128)(2,1)}), bf16[16,2,16,1,512]{4,2,1,3,0:T(8,128)(2,1)S(1)}, u32[]{:S(2)}, u32[]{:S(2)}) async-start(bf16[16,2,16,1,512]{4,2,1,3,0:T(8,128)(2,1)} %constant_dynamic-update-slice_fusion), calls=%async_computation.1 | async-start | bytes 1048576 | tf_op jit(solution)/shard_map/all_to_all | solution.py:61
  82.8 0.7 copy.63
  84.2 1.4 fusion.69
  85.5 15.7 %all-to-all-done.1 = bf16[16,2,16,1,512]{4,2,1,3,0:T(8,128)(2,1)S(1)} async-done(((bf16[16,2,16,1,512]{4,2,1,3,0:T(8,128)(2,1)}), bf16[16,2,16,1,512]{4,2,1,3,0:T(8,128)(2,1)S(1)}, u32[]{:S(2)}, u32[]{:S(2)}) %all-to-all-start.1) | async-done | bytes 524320 | tf_op jit(solution)/shard_map/all_to_all | solution.py:61
  101.2 0.8 copy-done.3
  102.0 3.5 %fusion.75 = (bf16[2,16,16,512]{3,1,0,2:T(8,128)(2,1)S(1)}, f32[2,16,16,512]{3,1,0,2:T(8,128)S(1)}) fusion(f32[2,16,16,512]{3,1,0,2:T(8,128)S(1)} %get-tuple-element.28, f32[1,16,16]{2,1,0:T(8,128)S(1)} %copy-done, f32[2,16,1,512]{3,1,0,2:T(8,128)} %copy-done.16, f32[2,16,1,512]{3,1,0,2:T(8,128)} %copy-done.17, bf16[16,2,16,1,512]{4,2,1,3,0:T(8,128)(2,1)} %copy-done.3, ...), kind=kOutput, calls=%fused_computation.173 | convolution fusion | flops 54525952 | bytes 6026240 | tf_op jit(solution)/shard_map/bac,fbcxy->fbaxy/dot_general | solution.py:85
  105.6 1.9 collective-permute-start.3
  107.5 4.5 %collective-permute-start.2 = (f32[2,16,1,512]{3,1,0,2:T(8,128)S(1)}, f32[2,16,1,512]{3,1,0,2:T(8,128)S(1)}, u32[]{:S(2)}, u32[]{:S(2)}) collective-permute-start(f32[2,16,1,512]{3,1,0,2:T(8,128)S(1)} %get-tuple-element.17), channel_id=1, source_target_pairs={{16,0},{32,16},{48,32},{64,48},{80,64},{96,80},{112,96},{128,112},... | collective-permute-start | bytes 196616 | tf_op jit(solution)/shard_map/ppermute | solution.py:19
  112.1 1.8 collective-permute-done.2
  116.7 45.6 %all_to_all.40 = bf16[2,3,16,16,512]{4,2,1,0,3:T(8,128)(2,1)S(1)} all-to-all(bf16[2,3,16,16,512]{4,2,1,0,3:T(8,128)(2,1)S(1)} %multiply_convert_fusion), channel_id=1, replica_groups=mesh['space'=32,'modes'=16] {'modes'}, dimensions={3} | all-to-all | bytes 3145728 | tf_op jit(solution)/shard_map/all_to_all | solution.py:59
  162.4 0.8 copy-done.5
  173.7 4.4 %all-to-all-start.3 = ((bf16[16,2,16,1,512]{4,2,1,3,0:T(8,128)(2,1)}), bf16[16,2,16,1,512]{4,2,1,3,0:T(8,128)(2,1)}, u32[]{:S(2)}, u32[]{:S(2)}) async-start(bf16[16,2,16,1,512]{4,2,1,3,0:T(8,128)(2,1)} %constant_dynamic-update-slice_fusion.16), calls=%async_computation.3 | async-start | bytes 1048576 | tf_op jit(solution)/shard_map/all_to_all | solution.py:61
  178.6 18.0 %all-to-all-done.3 = bf16[16,2,16,1,512]{4,2,1,3,0:T(8,128)(2,1)} async-done(((bf16[16,2,16,1,512]{4,2,1,3,0:T(8,128)(2,1)}), bf16[16,2,16,1,512]{4,2,1,3,0:T(8,128)(2,1)}, u32[]{:S(2)}, u32[]{:S(2)}) %all-to-all-start.3) | async-done | bytes 524320 | tf_op jit(solution)/shard_map/all_to_all | solution.py:61
  196.6 3.1 %fusion.1 = f32[2,16,16,512]{3,1,0,2:T(8,128)S(1)} fusion(f32[2,16,16,512]{3,1,0,2:T(8,128)S(1)} %get-tuple-element.46, f32[2,16,1,512]{3,1,0,2:T(8,128)S(1)} %copy-done.19, f32[2,16,1,512]{3,1,0,2:T(8,128)S(1)} %copy-done.21, f32[2,16,16,511]{3,1,0,2:T(8,128)S(1)} %get-tuple-element.16, f32[2,16,16,511]{3,1,0,2:T(8,128)S(1)} %get-tuple-element.15, ...), kind=kOutput, calls=%fused_computation.6 | convolution fusion | flops 54263808 | bytes 5501952 | tf_op jit(solution)/shard_map/bac,fbcxy->fbaxy/dot_general | solution.py:85
  199.7 1.6 copy.81
  (119 shorter events, 28.4 us)
Async XLA Ops:
  0.0 102.0 %copy-start = (f32[1,16,16]{2,1,0:T(8,128)S(1)}, f32[1,16,16]{2,1,0:T(8,128)}, u32[]{:S(2)}) copy-start(f32[1,16,16]{2,1,0:T(8,128)} %param.15) | copy-start | bytes 3076
  0.0 7.9 %copy-start.24 = (s32[16,512]{1,0:T(8,128)S(1)}, s32[16,512]{1,0:T(8,128)}, u32[]{:S(2)}) copy-start(s32[16,512]{1,0:T(8,128)} %param.10) | copy-start | bytes 98308
  0.0 8.0 %copy-start.22 = (f32[2,3,8]{2,0,1:T(2,128)S(1)}, f32[2,3,8]{2,0,1:T(2,128)}, u32[]{:S(2)}) copy-start(f32[2,3,8]{2,0,1:T(2,128)} %param.12) | copy-start | bytes 580
  1.5 7.8 %collective-permute-start.1 = (f32[2,16,1,512]{3,1,0,2:T(8,128)S(1)}, f32[2,16,1,512]{3,1,0,2:T(8,128)S(1)}, u32[]{:S(2)}, u32[]{:S(2)}) collective-permute-start(f32[2,16,1,512]{3,1,0,2:T(8,128)S(1)} %get-tuple-element.22), channel_id=1, source_target_pairs={{0,16},{16,32},{32,48},{48,64},{64,80},{80,96},{96,112},{112,128},... | collective-permute-start | bytes 196616 | tf_op jit(solution)/shard_map/ppermute | solution.py:16
  3.4 6.4 %collective-permute-start = (f32[2,16,1,512]{3,1,0,2:T(8,128)S(1)}, f32[2,16,1,512]{3,1,0,2:T(8,128)S(1)}, u32[]{:S(2)}, u32[]{:S(2)}) collective-permute-start(f32[2,16,1,512]{3,1,0,2:T(8,128)S(1)} %get-tuple-element.21), channel_id=1, source_target_pairs={{16,0},{32,16},{48,32},{64,48},{80,64},{96,80},{112,96},{128,112},... | collective-permute-start | bytes 196616 | tf_op jit(solution)/shard_map/ppermute | solution.py:19
  8.0 2.3 %copy-start.8 = (f32[16,512]{1,0:T(8,128)}, f32[16,512]{1,0:T(8,128)S(1)}, u32[]{:S(2)}) copy-start(f32[16,512]{1,0:T(8,128)S(1)} %get-tuple-element.33) | copy-start | bytes 98308
  8.0 2.3 %copy-start.10 = (f32[16,512]{1,0:T(8,128)}, f32[16,512]{1,0:T(8,128)S(1)}, u32[]{:S(2)}) copy-start(f32[16,512]{1,0:T(8,128)S(1)} %get-tuple-element.34) | copy-start | bytes 98308
  8.0 2.3 %copy-start.12 = (f32[16,512]{1,0:T(8,128)}, f32[16,512]{1,0:T(8,128)S(1)}, u32[]{:S(2)}) copy-start(f32[16,512]{1,0:T(8,128)S(1)} %get-tuple-element.35) | copy-start | bytes 98308
  8.0 2.3 %copy-start.14 = (f32[16,512]{1,0:T(8,128)}, f32[16,512]{1,0:T(8,128)S(1)}, u32[]{:S(2)}) copy-start(f32[16,512]{1,0:T(8,128)S(1)} %get-tuple-element.36) | copy-start | bytes 98308
  12.8 13.0 %copy-start.25 = (s32[3,16,16]{2,1,0:T(8,128)S(1)}, s32[3,16,16]{2,1,0:T(8,128)}, u32[]{:S(2)}) copy-start(s32[3,16,16]{2,1,0:T(8,128)} %param.14) | copy-start | bytes 9220
  12.8 54.5 %all-to-all-start = ((bf16[2,3,16,16,512]{4,2,1,0,3:T(8,128)(2,1)}), bf16[2,3,16,16,512]{4,2,1,0,3:T(8,128)(2,1)S(1)}, u32[]{:S(2)}, u32[]{:S(2)}) async-start(bf16[2,3,16,16,512]{4,2,1,0,3:T(8,128)(2,1)} %multiply_convert_fusion.1), calls=%async_computation | async-start | bytes 3145728 | tf_op jit(solution)/shard_map/all_to_all | solution.py:59
  68.9 13.5 %copy-start.23 = (f32[2,8]{1,0:T(2,128)S(1)}, f32[2,8]{1,0:T(2,128)}, u32[]{:S(2)}) copy-start(f32[2,8]{1,0:T(2,128)} %param.11) | copy-start | bytes 196
  68.9 13.7 %copy-start.9 = (f32[16,512]{1,0:T(8,128)S(1)}, f32[16,512]{1,0:T(8,128)}, u32[]{:S(2)}) copy-start(f32[16,512]{1,0:T(8,128)} %copy-done.8) | copy-start | bytes 98308
  68.9 13.7 %copy-start.11 = (f32[16,512]{1,0:T(8,128)S(1)}, f32[16,512]{1,0:T(8,128)}, u32[]{:S(2)}) copy-start(f32[16,512]{1,0:T(8,128)} %copy-done.10) | copy-start | bytes 98308
  68.9 13.7 %copy-start.13 = (f32[16,512]{1,0:T(8,128)S(1)}, f32[16,512]{1,0:T(8,128)}, u32[]{:S(2)}) copy-start(f32[16,512]{1,0:T(8,128)} %copy-done.12) | copy-start | bytes 98308
  68.9 13.7 %copy-start.15 = (f32[16,512]{1,0:T(8,128)S(1)}, f32[16,512]{1,0:T(8,128)}, u32[]{:S(2)}) copy-start(f32[16,512]{1,0:T(8,128)} %copy-done.14) | copy-start | bytes 98308
  78.8 22.5 %all-to-all-start.1 = ((bf16[16,2,16,1,512]{4,2,1,3,0:T(8,128)(2,1)}), bf16[16,2,16,1,512]{4,2,1,3,0:T(8,128)(2,1)S(1)}, u32[]{:S(2)}, u32[]{:S(2)}) async-start(bf16[16,2,16,1,512]{4,2,1,3,0:T(8,128)(2,1)} %constant_dynamic-update-slice_fusion), calls=%async_computation.1 | async-start | bytes 1048576 | tf_op jit(solution)/shard_map/all_to_all | solution.py:61
  105.6 6.5 %collective-permute-start.3 = (f32[2,16,1,512]{3,1,0,2:T(8,128)S(1)}, f32[2,16,1,512]{3,1,0,2:T(8,128)S(1)}, u32[]{:S(2)}, u32[]{:S(2)}) collective-permute-start(f32[2,16,1,512]{3,1,0,2:T(8,128)S(1)} %get-tuple-element.18), channel_id=1, source_target_pairs={{0,16},{16,32},{32,48},{48,64},{64,80},{80,96},{96,112},{112,128},... | collective-permute-start | bytes 196616 | tf_op jit(solution)/shard_map/ppermute | solution.py:16
  107.5 6.4 %collective-permute-start.2 = (f32[2,16,1,512]{3,1,0,2:T(8,128)S(1)}, f32[2,16,1,512]{3,1,0,2:T(8,128)S(1)}, u32[]{:S(2)}, u32[]{:S(2)}) collective-permute-start(f32[2,16,1,512]{3,1,0,2:T(8,128)S(1)} %get-tuple-element.17), channel_id=1, source_target_pairs={{16,0},{32,16},{48,32},{64,48},{80,64},{96,80},{112,96},{128,112},... | collective-permute-start | bytes 196616 | tf_op jit(solution)/shard_map/ppermute | solution.py:19
  173.7 22.8 %all-to-all-start.3 = ((bf16[16,2,16,1,512]{4,2,1,3,0:T(8,128)(2,1)}), bf16[16,2,16,1,512]{4,2,1,3,0:T(8,128)(2,1)}, u32[]{:S(2)}, u32[]{:S(2)}) async-start(bf16[16,2,16,1,512]{4,2,1,3,0:T(8,128)(2,1)} %constant_dynamic-update-slice_fusion.16), calls=%async_computation.3 | async-start | bytes 1048576 | tf_op jit(solution)/shard_map/all_to_all | solution.py:61
  178.2 18.4 %copy-start.6 = (f32[2,16,512]{2,0,1:T(2,128)S(1)}, f32[2,16,512]{2,0,1:T(2,128)}, u32[]{:S(2)}) copy-start(f32[2,16,512]{2,0,1:T(2,128)} %copy.63) | copy-start | bytes 196612
  178.2 18.4 %copy-start.7 = (f32[2,16,512]{2,0,1:T(2,128)S(1)}, f32[2,16,512]{2,0,1:T(2,128)}, u32[]{:S(2)}) copy-start(f32[2,16,512]{2,0,1:T(2,128)} %copy.74) | copy-start | bytes 196612
  178.2 18.4 %copy-start.19 = (f32[2,16,1,512]{3,1,0,2:T(8,128)S(1)}, f32[2,16,1,512]{3,1,0,2:T(8,128)}, u32[]{:S(2)}) copy-start(f32[2,16,1,512]{3,1,0,2:T(8,128)} %copy-done.18) | copy-start | bytes 196612
  178.2 18.4 %copy-start.21 = (f32[2,16,1,512]{3,1,0,2:T(8,128)S(1)}, f32[2,16,1,512]{3,1,0,2:T(8,128)}, u32[]{:S(2)}) copy-start(f32[2,16,1,512]{3,1,0,2:T(8,128)} %copy-done.20) | copy-start | bytes 196612
  (9 other events, 9.8 us)
